TPU v7x, 32 devices: a whole 2x2x4 slice. The times are simulated.
32 devices in a mesh: dp: 2 (over x), expert: 4 (over y, core), tensor: 4 (over z).
Axes of the slice: x: 2, y: 2, z: 4, core: 2. Of those that a mesh axis runs over, the one named last changes fastest.
Arguments:
- output_grad: bfloat16 [2048, 4096], P(('dp', 'expert'), 'tensor'), may hold values from -6 to 6
- expert_ids: int32 [2048, 2], P(('dp', 'expert')), may hold values from 0 to 3, all different within a row; in each aligned block of 256 rows (0 to 255, 256 to 511, ...) at most 192 rows name the same one
- router_weights: bfloat16 [2048, 2], P(('dp', 'expert')), may hold values from 0.099609375 to 0.8984375
- gate_preact: bfloat16 [4, 1536, 14336], P('expert', 'dp', 'tensor'), may hold values from -6 to 6
- up_preact: bfloat16 [4, 1536, 14336], P('expert', 'dp', 'tensor'), may hold values from -6 to 6
- down_weight: bfloat16 [4, 14336, 4096], P('expert', 'tensor', 'dp'), may hold values from -0.046875 to 0.046875
Outputs:
- gate_preact_grad: bfloat16 [4, 1536, 14336], P('expert', 'dp', 'tensor')
- up_preact_grad: bfloat16 [4, 1536, 14336], P('expert', 'dp', 'tensor')
- down_grad: bfloat16 [4, 14336, 4096], P('expert', 'tensor', 'dp')
- router_grad: float32 [2048, 2], P(('dp', 'expert'))
Inputs may be any that keep to these rules, and one draw needn't show every extreme that they name: `expert_ids`: the ids of one token differ. Among the 256 rows of one device no expert is named by more than 192 rows, and in every draw some expert is named by exactly 192 rows of some device.
All inputs are finite; a program needn't handle non-finite values.
Results may differ from a plain program's by a relative error of at most 0.007.
Values may be sent and summed in bfloat16 or wider, within the bound.
No kernel may reach another device: no remote copies, remote signals or barrier semaphores. Data moves between devices by JAX's collectives and lax.ppermute only.
A program may use at most 192 MiB of HBM per device.

v0:
```python
import jax
import jax.numpy as jnp
from jax import lax
from jax.sharding import PartitionSpec as P

PARTIAL_DTYPE = jnp.float32


def silu_parts(values):
    sigma = jax.nn.sigmoid(values)
    return (values * sigma, sigma * (1.0 + values * (1.0 - sigma)))


def swap_dp(value):
    return lax.ppermute(value, "dp", perm=[(0, 1), (1, 0)])


def local(output_grad, expert_ids, router_weights, gate_preact, up_preact, down_weight):
    expert_count = lax.axis_size("expert")
    tensor_count = lax.axis_size("tensor")
    replica = lax.axis_index("dp")
    part = lax.axis_index("tensor")
    tokens_here = expert_ids.shape[0]
    choices_each = expert_ids.shape[1]
    capacity = gate_preact.shape[1] // expert_count
    flat_ids = expert_ids.reshape(-1)
    one_hot = (flat_ids[:, None] == jnp.arange(expert_count, dtype=jnp.int32)).astype(jnp.int32)
    earlier = jnp.cumsum(one_hot, axis=0) - one_hot
    slot_index = jnp.sum(earlier * one_hot, axis=1)
    target = (flat_ids * capacity + slot_index).reshape(tokens_here, choices_each)
    columns = jnp.arange(expert_count * capacity, dtype=jnp.int32)
    matches = [target[:, which][:, None] == columns[None, :] for which in range(choices_each)]
    selector = jnp.zeros((tokens_here, expert_count * capacity), jnp.bfloat16)
    gate_table = jnp.zeros((tokens_here, expert_count * capacity), jnp.float32)
    for which in range(choices_each):
        selector = jnp.where(matches[which], jnp.bfloat16(1.0), selector)
        gate_table = jnp.where(
            matches[which], router_weights[:, which : which + 1].astype(jnp.float32), gate_table
        )
    gate_send = jnp.sum(gate_table, axis=0).astype(jnp.bfloat16).reshape(expert_count, capacity)
    gate_float = gate_preact[0].astype(jnp.float32)
    up_float = up_preact[0].astype(jnp.float32)
    active, slope = silu_parts(gate_float)
    hidden = (active * up_float).astype(jnp.bfloat16)
    contract_rows = (((0,), (0,)), ((), ()))
    contract_cols = (((1,), (1,)), ((), ()))
    outgoing = lax.dot_general(
        selector, output_grad, contract_rows, preferred_element_type=jnp.float32
    )
    outgoing = outgoing.astype(jnp.bfloat16).reshape(expert_count, capacity, -1)
    hidden, outgoing = lax.optimization_barrier((hidden, outgoing))
    hidden_other = swap_dp(hidden)
    received = lax.all_to_all(outgoing, "expert", split_axis=0, concat_axis=0, tiled=True)
    gate_slots = lax.all_to_all(gate_send, "expert", split_axis=0, concat_axis=0, tiled=True)
    slots = expert_count * capacity
    narrow_rows = received.reshape(slots, -1)
    gate_bf16 = gate_slots.reshape(-1)
    gate_column = gate_bf16.astype(jnp.float32)[:, None]
    fragment = lax.all_gather(narrow_rows, "tensor", axis=1, tiled=True)
    width = fragment.shape[1]
    half = width // 2
    piece = half // tensor_count
    own_rows = lax.dynamic_slice_in_dim(fragment, replica * half, half, axis=1)
    send_rows = lax.dynamic_slice_in_dim(
        fragment, (1 - replica) * half + part * piece, piece, axis=1
    )
    other_piece = swap_dp(send_rows)
    other_rows = lax.all_gather(other_piece, "tensor", axis=1, tiled=True)
    hidden_other, other_rows = lax.optimization_barrier((hidden_other, other_rows))
    other_gates = swap_dp(gate_bf16).astype(jnp.float32)[:, None]
    local_weight = down_weight[0]
    partial_other = lax.dot_general(
        other_rows, local_weight, contract_cols, preferred_element_type=jnp.float32
    )
    partial_back = swap_dp(partial_other.astype(PARTIAL_DTYPE)).astype(jnp.float32)
    partial_own = lax.dot_general(
        own_rows, local_weight, contract_cols, preferred_element_type=jnp.float32
    )
    scaled_own = (gate_column * own_rows.astype(jnp.float32)).astype(jnp.bfloat16)
    scaled_other = (other_gates * other_rows.astype(jnp.float32)).astype(jnp.bfloat16)
    grad_own = lax.dot_general(
        hidden, scaled_own, contract_rows, preferred_element_type=jnp.float32
    )
    grad_other = lax.dot_general(
        hidden_other, scaled_other, contract_rows, preferred_element_type=jnp.float32
    )
    rounded_own = lax.optimization_barrier(grad_own.astype(jnp.bfloat16))
    rounded_other = lax.optimization_barrier(grad_other.astype(jnp.bfloat16))
    partial_back, rounded_own, rounded_other = lax.optimization_barrier(
        (partial_back, rounded_own, rounded_other)
    )
    upstream = partial_own + partial_back
    down_grad = (rounded_own.astype(jnp.float32) + rounded_other.astype(jnp.float32)).astype(
        jnp.bfloat16
    )
    score = jnp.sum(hidden.astype(jnp.float32) * upstream, axis=1)
    hidden_grad = gate_column * upstream
    gate_grad = (hidden_grad * up_float * slope).astype(jnp.bfloat16)
    up_grad = (hidden_grad * active).astype(jnp.bfloat16)
    summed_scores = lax.psum(score, "tensor")
    returned = lax.all_to_all(
        summed_scores.reshape(expert_count, capacity),
        "expert",
        split_axis=0,
        concat_axis=0,
        tiled=True,
    )
    flat_scores = returned.reshape(-1)
    router_grad = jnp.stack(
        [
            jnp.sum(jnp.where(matches[which], flat_scores[None, :], 0.0), axis=1)
            for which in range(choices_each)
        ],
        axis=1,
    )
    return (gate_grad[None], up_grad[None], down_grad[None], router_grad)


def solution(mesh):
    placed = (
        P(("dp", "expert"), "tensor"),
        P(("dp", "expert"), None),
        P(("dp", "expert"), None),
        P("expert", "dp", "tensor"),
        P("expert", "dp", "tensor"),
        P("expert", "tensor", "dp"),
    )
    return jax.shard_map(
        local,
        mesh=mesh,
        in_specs=placed,
        out_specs=(
            P("expert", "dp", "tensor"),
            P("expert", "dp", "tensor"),
            P("expert", "tensor", "dp"),
            P(("dp", "expert"), None),
        ),
        check_vma=False,
    )
```

profile of v0, /device:TPU:1, one launch (start us, length us, event | category | flops | bytes accessed | tf_op | source)
XLA Modules:
  0.0 616.6 jit_solution(12437453717802722302)
XLA Ops:
  7.2 0.9 copy.28
  8.4 1.2 reduce-window.6
  10.3 0.7 multiply_add_fusion
  11.1 8.8 %fusion.5 = bf16[768,3584]{1,0:T(8,128)(2,1)} fusion(bf16[1,768,3584]{2,1,0:T(8,128)(2,1)} %param.10, bf16[1,768,3584]{2,1,0:T(8,128)(2,1)} %param.9), kind=kLoop, calls=%fused_computation.13 | loop fusion | flops 22020096 | bytes 16515072 | tf_op jit(solution)/shard_map/convert_element_type | solution.py:44
  19.9 0.8 convolution_convert_fusion.2
  20.7 23.2 %all_to_all.20 = bf16[4,192,1024]{2,1,0:T(8,128)(2,1)} all-to-all(bf16[4,192,1024]{2,1,0:T(8,128)(2,1)S(1)} %bitcast.61), channel_id=1, replica_groups=mesh['dp'=2,'expert'=4,'tensor'=4] {'expert'}, dimensions={0} | all-to-all | bytes 3145728 | tf_op jit(solution)/shard_map/all_to_all | solution.py:53
  44.0 1.8 collective-permute-start
  45.7 115.1 %all-gather.3.cloned.1.call-done = bf16[768,4096]{1,0:T(8,128)(2,1)} async-done(((bf16[768,1024]{1,0:T(8,128)(2,1)}), bf16[768,4096]{1,0:T(8,128)(2,1)}) %all-gather.3.cloned.1.call-update) | async-done | bytes 6291472 | tf_op jit(solution)/shard_map/all_gather | solution.py:59
  160.8 1.2 constant_dynamic-slice_fusion
  162.0 1.2 collective-permute-start.1
  163.2 18.3 %collective-permute-done.1 = bf16[768,512]{1,0:T(8,128)(2,1)S(1)} collective-permute-done((bf16[768,512]{1,0:T(8,128)(2,1)S(1)}, bf16[768,512]{1,0:T(8,128)(2,1)S(1)}, u32[]{:S(2)}, u32[]{:S(2)}) %collective-permute-start.1) | collective-permute-done | bytes 786464 | tf_op jit(solution)/shard_map/ppermute | solution.py:15
  181.5 0.9 copy-done.2
  182.5 64.6 %all-gather.5.cloned.1.call-done = bf16[768,2048]{1,0:T(8,128)(2,1)} async-done(((bf16[768,512]{1,0:T(8,128)(2,1)}), bf16[768,2048]{1,0:T(8,128)(2,1)}) %all-gather.5.cloned.1.call-update) | async-done | bytes 3145744 | tf_op jit(solution)/shard_map/all_gather | solution.py:68
  247.0 18.2 %fusion.1 = f32[768,3584]{1,0:T(8,128)} fusion(bf16[768,2048]{1,0:T(8,128)(2,1)} %all-gather.5.cloned.1.call-done, bf16[1,3584,2048]{2,1,0:T(8,128)(2,1)} %param.11), kind=kOutput, calls=%fused_computation.7 | convolution fusion | flops 11274289152 | bytes 28835840 | tf_op jit(solution)/shard_map/dot_general | solution.py:72
  265.2 1.2 collective-permute-start.2
  266.7 7.0 %all_to_all.21 = bf16[4,1,192]{2,1,0:T(2,128)(2,1)S(1)} all-to-all(bf16[4,1,192]{2,1,0:T(2,128)(2,1)S(1)} %convert_element_type.113), channel_id=1, replica_groups=mesh['dp'=2,'expert'=4,'tensor'=4] {'expert'}, dimensions={0} | all-to-all | bytes 3072 | tf_op jit(solution)/shard_map/all_to_all | solution.py:54
  274.1 229.0 %collective-permute-done.3 = bf16[768]{0:T(1024)(128)(2,1)S(1)} collective-permute-done((bf16[768]{0:T(1024)(128)(2,1)S(1)}, bf16[768]{0:T(1024)(128)(2,1)S(1)}, u32[]{:S(2)}, u32[]{:S(2)}) %collective-permute-start.3) | collective-permute-done | bytes 1568 | tf_op jit(solution)/shard_map/ppermute | solution.py:15
  503.1 18.3 %convolution_convert_fusion.1 = bf16[3584,2048]{1,0:T(8,128)(2,1)} fusion(bf16[768,3584]{1,0:T(8,128)(2,1)} %fusion.5, f32[768]{0:T(1024)S(1)} %convert_element_type.91, bf16[768,4096]{1,0:T(8,128)(2,1)} %all-gather.3.cloned.1.call-done, s32[]{:T(128)S(6)} %select_n.31), kind=kOutput, calls=%fused_computation.5 | convolution fusion | flops 11286347776 | bytes 23333892 | tf_op jit(solution)/shard_map/dot_general | solution.py:81
  521.3 18.3 %fusion.3 = f32[768,3584]{1,0:T(8,128)} fusion(bf16[1,3584,2048]{2,1,0:T(8,128)(2,1)} %param.11, bf16[768,4096]{1,0:T(8,128)(2,1)} %all-gather.3.cloned.1.call-done, s32[]{:T(128)S(6)} %select_n.31), kind=kOutput, calls=%fused_computation.9 | convolution fusion | flops 11274289152 | bytes 28835844 | tf_op jit(solution)/shard_map/dot_general | solution.py:76
  539.6 17.9 %convolution_convert_fusion = bf16[3584,2048]{1,0:T(8,128)(2,1)} fusion(bf16[768,3584]{1,0:T(8,128)(2,1)} %collective-permute-done, bf16[768,2048]{1,0:T(8,128)(2,1)} %all-gather.5.cloned.1.call-done, f32[768]{0:T(1024)S(1)} %convert_element_type.101), kind=kOutput, calls=%fused_computation.4 | convolution fusion | flops 11286347776 | bytes 23333888 | tf_op jit(solution)/shard_map/dot_general | solution.py:84
  557.5 17.8 %fusion.13 = (bf16[1,768,3584]{2,1,0:T(8,128)(2,1)}, bf16[1,768,3584]{2,1,0:T(8,128)(2,1)}, f32[768]{0:T(1024)S(1)}) fusion(f32[768]{0:T(1024)S(1)} %convert_element_type.91, bf16[1,768,3584]{2,1,0:T(8,128)(2,1)S(1)} %bitcast.59, f32[768,3584]{1,0:T(8,128)} %fusion.3, f32[768,3584]{1,0:T(8,128)} %collective-permute-done.2, bf16[1,768,3584]{2,1,0:T(8,128)(2,1)} %param.10, ...), kind=kLoop, calls=%fused_computation.25 | loop fusion | flops 55049472 | bytes 49551360 | tf_op jit(solution)/shard_map/broadcast_in_dim | solution.py:116
  575.4 8.4 %psum.7 = f32[4,1,192]{2,1,0:T(1,128)} all-reduce(f32[4,1,192]{2,1,0:T(1,128)S(1)} %all_to_all.15), channel_id=1, replica_groups=mesh['dp'=2,'expert'=4,'tensor'=4] {'tensor'}, use_global_device_ids=true, to_apply=%region_5.6 | all-reduce | flops 768 | bytes 6144 | tf_op jit(solution)/shard_map/psum | solution.py:100
  583.9 6.2 %all-to-all-start.2 = ((f32[4,1,192]{2,1,0:T(1,128)}), f32[4,1,192]{2,1,0:T(1,128)S(1)}, u32[]{:S(2)}, u32[]{:S(2)}) async-start(f32[4,1,192]{2,1,0:T(1,128)} %psum.7), calls=%async_computation.2 | async-start | bytes 8192 | tf_op jit(solution)/shard_map/all_to_all | solution.py:101
  590.1 18.7 %fusion = bf16[1,3584,2048]{2,1,0:T(8,128)(2,1)} fusion(bf16[3584,2048]{1,0:T(8,128)(2,1)} %convolution_convert_fusion, bf16[3584,2048]{1,0:T(8,128)(2,1)} %convolution_convert_fusion.1), kind=kLoop, calls=%fused_computation.6 | loop fusion | flops 29360128 | bytes 44040192 | tf_op jit(solution)/shard_map/broadcast_in_dim | solution.py:116
  (42 shorter events, 3.0 us)
Async XLA Ops:
  7.2 12.7 %copy-start = (bf16[256,1024]{1,0:T(8,128)(2,1)S(1)}, bf16[256,1024]{1,0:T(8,128)(2,1)}, u32[]{:S(2)}) copy-start(bf16[256,1024]{1,0:T(8,128)(2,1)} %param.6) | copy-start | bytes 1572868
  7.2 153.6 %all-gather.3.cloned.1.call-start = ((), (), s32[]{:S(2)}) async-start(), calls=%async_computation.3 | async-start | bytes 7864320 | tf_op jit(solution)/shard_map/all_gather | solution.py:59
  43.9 203.1 %all-gather.5.cloned.1.call-start = ((), (), s32[]{:S(2)}) async-start(), calls=%async_computation.4 | async-start | bytes 3932160 | tf_op jit(solution)/shard_map/all_gather | solution.py:68
  44.0 138.5 %collective-permute-start = (bf16[768,3584]{1,0:T(8,128)(2,1)}, bf16[768,3584]{1,0:T(8,128)(2,1)}, u32[]{:S(2)}, u32[]{:S(2)}) collective-permute-start(bf16[768,3584]{1,0:T(8,128)(2,1)} %fusion.5), channel_id=1, source_target_pairs={{0,16},{16,0},{1,17},{17,1},{2,18},{18,2},{3,19},{19,3},{4,20},{20... | collective-permute-start | bytes 16515080 | tf_op jit(solution)/shard_map/ppermute | solution.py:15
  162.0 19.6 %collective-permute-start.1 = (bf16[768,512]{1,0:T(8,128)(2,1)S(1)}, bf16[768,512]{1,0:T(8,128)(2,1)S(1)}, u32[]{:S(2)}, u32[]{:S(2)}) collective-permute-start(bf16[768,512]{1,0:T(8,128)(2,1)S(1)} %constant_dynamic-slice_fusion), channel_id=1, source_target_pairs={{0,16},{16,0},{1,17},{17,1},{2,18},{18,2},{3,19},{19,3},{4,20},{20... | collective-permute-start | bytes 2359304 | tf_op jit(solution)/shard_map/ppermute | solution.py:15
  181.5 0.9 copy-start.2
  182.4 83.9 %copy-start.3 = (bf16[256,2]{0,1:T(2,128)(2,1)S(1)}, bf16[256,2]{0,1:T(2,128)(2,1)}, u32[]{:S(2)}) copy-start(bf16[256,2]{0,1:T(2,128)(2,1)} %param.8) | copy-start | bytes 3076
  265.2 292.3 %collective-permute-start.2 = (f32[768,3584]{1,0:T(8,128)}, f32[768,3584]{1,0:T(8,128)}, u32[]{:S(2)}, u32[]{:S(2)}) collective-permute-start(f32[768,3584]{1,0:T(8,128)} %fusion.1), channel_id=1, source_target_pairs={{0,16},{16,0},{1,17},{17,1},{2,18},{18,2},{3,19},{19,3},{4,20},{20... | collective-permute-start | bytes 33030152 | tf_op jit(solution)/shard_map/ppermute | solution.py:15
  273.8 229.3 %collective-permute-start.3 = (bf16[768]{0:T(1024)(128)(2,1)S(1)}, bf16[768]{0:T(1024)(128)(2,1)S(1)}, u32[]{:S(2)}, u32[]{:S(2)}) collective-permute-start(bf16[768]{0:T(1024)(128)(2,1)S(1)} %reshape.71), channel_id=1, source_target_pairs={{0,16},{16,0},{1,17},{17,1},{2,18},{18,2},{3,19},{19,3},{4,20},{20... | collective-permute-start | bytes 4616 | tf_op jit(solution)/shard_map/ppermute | solution.py:15
  503.1 54.5 %slice-start = ((s8[5505024]{0:T(1024)(128)(4,1)}), s8[4194304]{0:T(1024)(128)(4,1)S(1)}, s32[]{:S(2)}) async-start(s8[5505024]{0:T(1024)(128)(4,1)} %bitcast.58), calls=%async_computation.5 | async-start | bytes 8388608
  521.3 36.2 %slice-start.1 = ((s8[5505024]{0:T(1024)(128)(4,1)}), s8[1310720]{0:T(1024)(128)(4,1)S(1)}, s32[]{:S(2)}) async-start(s8[5505024]{0:T(1024)(128)(4,1)} %bitcast.58), calls=%async_computation.6 | async-start | bytes 2621440
  583.9 24.9 %all-to-all-start.2 = ((f32[4,1,192]{2,1,0:T(1,128)}), f32[4,1,192]{2,1,0:T(1,128)S(1)}, u32[]{:S(2)}, u32[]{:S(2)}) async-start(f32[4,1,192]{2,1,0:T(1,128)} %psum.7), calls=%async_computation.2 | async-start | bytes 8192 | tf_op jit(solution)/shard_map/all_to_all | solution.py:101
  590.1 19.7 %copy-start.1 = (bf16[256,1024]{1,0:T(8,128)(2,1)S(1)}, bf16[256,1024]{1,0:T(8,128)(2,1)}, u32[]{:S(2)}) copy-start(bf16[256,1024]{1,0:T(8,128)(2,1)} %param.6) | copy-start | bytes 1572868
Sparse Core Ops, SparseCore 0:
  44.1 116.7 all-gather.2
  182.6 64.4 all-gather.4
where the time goes:
time: 617 us
  waiting for transfers between devices  427 us (69%)
  matrix products  73.4 us (12%)
  other arithmetic  48.8 us (8%)
  blocking collectives  38.6 us (6%)
  between operations  14.1 us (2%)
  starting transfers between devices  10.7 us (2%)
    ppermute x4, waiting for transfers between devices, swap_dp(): return lax.ppermute(value, 'dp', perm=[(0, 1), (1, 0)])  247 us
    all_gather x1, waiting for transfers between devices, local(): fragment = lax.all_gather(narrow_rows, 'tensor', axis=1, tiled=True)  115 us
    all_gather x1, waiting for transfers between devices, local(): other_rows = lax.all_gather(other_piece, 'tensor', axis=1, tiled=True)  64.6 us
    broadcast_in_dim x2, other arithmetic, local(): return (gate_grad[None], up_grad[None], down_grad[None], router_grad)  36.5 us
    all_to_all x1, blocking collectives, local(): lax.all_to_all(outgoing, 'expert', split_axis=0, concat_axis=0, tiled=True)  23.2 us
    dot_general x1, matrix products, local(): lax.dot_general(own_rows, local_weight, contract_cols, preferred_element_...  18.3 us
    dot_general x1, matrix products, local(): lax.dot_general(hidden, scaled_own, contract_rows, preferred_element_type...  18.3 us
    dot_general x1, matrix products, local(): lax.dot_general(other_rows, local_weight, contract_cols, preferred_elemen...  18.2 us
  transfers between devices with their start and end apart: 7, of which 4 were waited for; matrix products, arithmetic and copies ran while one was open for 12% of the time, Pallas kernels for 0%

commit v1 on v0

--- a/solution.py
+++ b/solution.py
@@ -65,7 +65,23 @@
         fragment, (1 - replica) * half + part * piece, piece, axis=1
     )
     other_piece = swap_dp(send_rows)
-    other_rows = lax.all_gather(other_piece, "tensor", axis=1, tiled=True)
+    ways, here, step = (lax.axis_size("tensor"), lax.axis_index("tensor"), other_piece.shape[1])
+    shape = [n * ways if d == 1 else n for d, n in enumerate(other_piece.shape)]
+    full = lax.dynamic_update_slice_in_dim(
+        jnp.zeros(shape, other_piece.dtype), other_piece, here * step, axis=1
+    )
+    going_up = going_down = other_piece
+    for far in range(1, ways // 2 + 1):
+        going_up = lax.ppermute(going_up, "tensor", [(d, (d + 1) % ways) for d in range(ways)])
+        full = lax.dynamic_update_slice_in_dim(full, going_up, (here - far) % ways * step, axis=1)
+        if 2 * far < ways:
+            going_down = lax.ppermute(
+                going_down, "tensor", [(d, (d - 1) % ways) for d in range(ways)]
+            )
+            full = lax.dynamic_update_slice_in_dim(
+                full, going_down, (here + far) % ways * step, axis=1
+            )
+    other_rows = full
     hidden_other, other_rows = lax.optimization_barrier((hidden_other, other_rows))
     other_gates = swap_dp(gate_bf16).astype(jnp.float32)[:, None]
     local_weight = down_weight[0]

time: 617 us -> 603 us (0.977)
  waiting for transfers between devices: 427 us -> 406 us
    all_gather x1 -> x0, waiting for transfers between devices: 64.6 us -> none  [local(): other_rows = lax.all_gather(other_piece, 'tensor', axis=1, tiled=True)]
    ppermute x0 -> x3, waiting for transfers between devices: none -> 47.6 us  [the longest x2 32.6 us: local(): lax.ppermute(going_up, 'tensor', [(d, (d + 1) % ways) for d in range(ways)])]
  transfers between devices with their start and end apart: 7 -> 9, of which waited for: 4 -> 6; matrix products, arithmetic and copies ran while one was open for 12% -> 13% of each run, Pallas kernels for 0% -> 0%
where the time goes in v1:
time: 603 us; the launch traced here: 602 us
  waiting for transfers between devices  406 us (67%)
  matrix products  72.7 us (12%)
  other arithmetic  48.8 us (8%)
  blocking collectives  39.1 us (6%)
  starting transfers between devices  16.5 us (3%)
  between operations  14.2 us (2%)
    ppermute x4, waiting for transfers between devices, swap_dp(): return lax.ppermute(value, 'dp', perm=[(0, 1), (1, 0)])  243 us
    all_gather x1, waiting for transfers between devices, local(): fragment = lax.all_gather(narrow_rows, 'tensor', axis=1, tiled=True)  115 us
    broadcast_in_dim x2, other arithmetic, local(): return (gate_grad[None], up_grad[None], down_grad[None], router_grad)  36.5 us
    ppermute x2, waiting for transfers between devices, local(): lax.ppermute(going_up, 'tensor', [(d, (d + 1) % ways) for d in range(ways)])  32.6 us
    all_to_all x1, blocking collectives, local(): lax.all_to_all(outgoing, 'expert', split_axis=0, concat_axis=0, tiled=True)  23.2 us
    dot_general x1, matrix products, local(): lax.dot_general(other_rows, local_weight, contract_cols, preferred_elemen...  18.4 us
    dot_general x1, matrix products, local(): lax.dot_general(own_rows, local_weight, contract_cols, preferred_element_...  18.4 us
    dot_general x1, matrix products, local(): lax.dot_general(hidden, scaled_own, contract_rows, preferred_element_type...  18.3 us
  transfers between devices with their start and end apart: 9, of which 6 were waited for; matrix products, arithmetic and copies ran while one was open for 13% of the time, Pallas kernels for 0%

profile of v1, /device:TPU:1, one launch (start us, length us, event | category | flops | bytes accessed | tf_op | source)
XLA Modules:
  0.0 602.5 jit_solution(4797667077214926300)
XLA Ops:
  8.4 1.2 reduce-window.6
  11.1 8.8 %fusion.5 = bf16[768,3584]{1,0:T(8,128)(2,1)} fusion(bf16[1,768,3584]{2,1,0:T(8,128)(2,1)} %param.10, bf16[1,768,3584]{2,1,0:T(8,128)(2,1)} %param.9), kind=kLoop, calls=%fused_computation.13 | loop fusion | flops 22020096 | bytes 16515072 | tf_op jit(solution)/shard_map/convert_element_type | solution.py:44
  20.7 23.2 %all_to_all.20 = bf16[4,192,1024]{2,1,0:T(8,128)(2,1)} all-to-all(bf16[4,192,1024]{2,1,0:T(8,128)(2,1)S(1)} %bitcast.61), channel_id=1, replica_groups=mesh['dp'=2,'expert'=4,'tensor'=4] {'expert'}, dimensions={0} | all-to-all | bytes 3145728 | tf_op jit(solution)/shard_map/all_to_all | solution.py:53
  43.9 1.8 collective-permute-start
  45.7 115.1 %all-gather.2.cloned.1.call-done = bf16[768,4096]{1,0:T(8,128)(2,1)} async-done(((bf16[768,1024]{1,0:T(8,128)(2,1)}), bf16[768,4096]{1,0:T(8,128)(2,1)}) %all-gather.2.cloned.1.call-update) | async-done | bytes 6291472 | tf_op jit(solution)/shard_map/all_gather | solution.py:59
  160.8 1.2 constant_dynamic-slice_fusion
  162.0 1.2 collective-permute-start.1
  163.2 18.2 %collective-permute-done.1 = bf16[768,512]{1,0:T(8,128)(2,1)S(1)} collective-permute-done((bf16[768,512]{1,0:T(8,128)(2,1)S(1)}, bf16[768,512]{1,0:T(8,128)(2,1)S(1)}, u32[]{:S(2)}, u32[]{:S(2)}) %collective-permute-start.1) | collective-permute-done | bytes 786464 | tf_op jit(solution)/shard_map/ppermute | solution.py:15
  182.0 2.8 collective-permute-start.3
  184.7 16.7 %collective-permute-done.2 = bf16[768,512]{1,0:T(8,128)(2,1)S(1)} collective-permute-done((bf16[768,512]{1,0:T(8,128)(2,1)S(1)}, bf16[768,512]{1,0:T(8,128)(2,1)S(1)}, u32[]{:S(2)}, u32[]{:S(2)}) %collective-permute-start.2) | collective-permute-done | bytes 786464 | tf_op jit(solution)/shard_map/ppermute | solution.py:75
  202.0 14.9 %collective-permute-done.3 = bf16[768,512]{1,0:T(8,128)(2,1)} collective-permute-done((bf16[768,512]{1,0:T(8,128)(2,1)S(1)}, bf16[768,512]{1,0:T(8,128)(2,1)}, u32[]{:S(2)}, u32[]{:S(2)}) %collective-permute-start.3) | collective-permute-done | bytes 786464 | tf_op jit(solution)/shard_map/ppermute | solution.py:78
  217.0 1.2 constant_dynamic-update-slice_fusion.1
  218.2 15.9 %collective-permute-done.4 = bf16[768,512]{1,0:T(8,128)(2,1)S(1)} collective-permute-done((bf16[768,512]{1,0:T(8,128)(2,1)S(1)}, bf16[768,512]{1,0:T(8,128)(2,1)S(1)}, u32[]{:S(2)}, u32[]{:S(2)}) %collective-permute-start.4) | collective-permute-done | bytes 786464 | tf_op jit(solution)/shard_map/ppermute | solution.py:75
  234.3 18.4 %fusion.1 = f32[768,3584]{1,0:T(8,128)} fusion(bf16[768,2048]{1,0:T(8,128)(2,1)S(1)} %constant_dynamic-update-slice_fusion, bf16[1,3584,2048]{2,1,0:T(8,128)(2,1)} %param.11), kind=kOutput, calls=%fused_computation.7 | convolution fusion | flops 11274289152 | bytes 28835840 | tf_op jit(solution)/shard_map/dot_general | solution.py:88
  252.7 1.6 collective-permute-start.5
  254.6 8.7 %all_to_all.21 = bf16[4,1,192]{2,1,0:T(2,128)(2,1)S(1)} all-to-all(bf16[4,1,192]{2,1,0:T(2,128)(2,1)S(1)} %convert_element_type.113), channel_id=1, replica_groups=mesh['dp'=2,'expert'=4,'tensor'=4] {'expert'}, dimensions={0} | all-to-all | bytes 3072 | tf_op jit(solution)/shard_map/all_to_all | solution.py:54
  263.5 225.2 %collective-permute-done.6 = bf16[768]{0:T(1024)(128)(2,1)S(1)} collective-permute-done((bf16[768]{0:T(1024)(128)(2,1)S(1)}, bf16[768]{0:T(1024)(128)(2,1)S(1)}, u32[]{:S(2)}, u32[]{:S(2)}) %collective-permute-start.6) | collective-permute-done | bytes 1568 | tf_op jit(solution)/shard_map/ppermute | solution.py:15
  488.7 18.3 %convolution_convert_fusion.1 = bf16[3584,2048]{1,0:T(8,128)(2,1)} fusion(bf16[768,3584]{1,0:T(8,128)(2,1)} %fusion.5, f32[768]{0:T(1024)S(1)} %convert_element_type.91, bf16[768,4096]{1,0:T(8,128)(2,1)} %all-gather.2.cloned.1.call-done, s32[]{:T(128)S(6)} %select_n.58), kind=kOutput, calls=%fused_computation.5 | convolution fusion | flops 11286347776 | bytes 23333892 | tf_op jit(solution)/shard_map/dot_general | solution.py:97
  507.0 18.4 %fusion.3 = f32[768,3584]{1,0:T(8,128)} fusion(bf16[1,3584,2048]{2,1,0:T(8,128)(2,1)} %param.11, bf16[768,4096]{1,0:T(8,128)(2,1)} %all-gather.2.cloned.1.call-done, s32[]{:T(128)S(6)} %select_n.58), kind=kOutput, calls=%fused_computation.9 | convolution fusion | flops 11274289152 | bytes 28835844 | tf_op jit(solution)/shard_map/dot_general | solution.py:92
  525.4 17.0 %convolution_convert_fusion = bf16[3584,2048]{1,0:T(8,128)(2,1)} fusion(bf16[768,3584]{1,0:T(8,128)(2,1)} %collective-permute-done, bf16[768,2048]{1,0:T(8,128)(2,1)S(1)} %copy-done.3, f32[768]{0:T(1024)S(1)} %convert_element_type.101), kind=kOutput, calls=%fused_computation.4 | convolution fusion | flops 11286347776 | bytes 23333888 | tf_op jit(solution)/shard_map/dot_general | solution.py:100
  542.3 17.8 %fusion.13 = (bf16[1,768,3584]{2,1,0:T(8,128)(2,1)}, bf16[1,768,3584]{2,1,0:T(8,128)(2,1)}, f32[768]{0:T(1024)S(1)}) fusion(f32[768]{0:T(1024)S(1)} %convert_element_type.91, bf16[1,768,3584]{2,1,0:T(8,128)(2,1)S(1)} %bitcast.59, f32[768,3584]{1,0:T(8,128)} %fusion.3, f32[768,3584]{1,0:T(8,128)} %collective-permute-done.5, bf16[1,768,3584]{2,1,0:T(8,128)(2,1)} %param.10, ...), kind=kLoop, calls=%fused_computation.25 | loop fusion | flops 55049472 | bytes 49551360 | tf_op jit(solution)/shard_map/broadcast_in_dim | solution.py:132
  560.2 7.2 %psum.7 = f32[4,1,192]{2,1,0:T(1,128)} all-reduce(f32[4,1,192]{2,1,0:T(1,128)S(1)} %all_to_all.15), channel_id=1, replica_groups=mesh['dp'=2,'expert'=4,'tensor'=4] {'tensor'}, use_global_device_ids=true, to_apply=%region_5.6 | all-reduce | flops 768 | bytes 6144 | tf_op jit(solution)/shard_map/psum | solution.py:116
  567.4 8.5 %all-to-all-start.2 = ((f32[4,1,192]{2,1,0:T(1,128)}), f32[4,1,192]{2,1,0:T(1,128)S(1)}, u32[]{:S(2)}, u32[]{:S(2)}) async-start(f32[4,1,192]{2,1,0:T(1,128)} %psum.7), calls=%async_computation.2 | async-start | bytes 8192 | tf_op jit(solution)/shard_map/all_to_all | solution.py:117
  575.9 18.7 %fusion = bf16[1,3584,2048]{2,1,0:T(8,128)(2,1)} fusion(bf16[3584,2048]{1,0:T(8,128)(2,1)} %convolution_convert_fusion, bf16[3584,2048]{1,0:T(8,128)(2,1)} %convolution_convert_fusion.1), kind=kLoop, calls=%fused_computation.6 | loop fusion | flops 29360128 | bytes 44040192 | tf_op jit(solution)/shard_map/broadcast_in_dim | solution.py:132
  (52 shorter events, 6.2 us)
Async XLA Ops:
  7.2 12.7 %copy-start = (bf16[256,1024]{1,0:T(8,128)(2,1)S(1)}, bf16[256,1024]{1,0:T(8,128)(2,1)}, u32[]{:S(2)}) copy-start(bf16[256,1024]{1,0:T(8,128)(2,1)} %param.6) | copy-start | bytes 1572868
  7.2 153.6 %all-gather.2.cloned.1.call-start = ((), (), s32[]{:S(2)}) async-start(), calls=%async_computation.3 | async-start | bytes 7864320 | tf_op jit(solution)/shard_map/all_gather | solution.py:59
  43.9 190.3 %collective-permute-start = (bf16[768,3584]{1,0:T(8,128)(2,1)}, bf16[768,3584]{1,0:T(8,128)(2,1)}, u32[]{:S(2)}, u32[]{:S(2)}) collective-permute-start(bf16[768,3584]{1,0:T(8,128)(2,1)} %fusion.5), channel_id=1, source_target_pairs={{0,16},{16,0},{1,17},{17,1},{2,18},{18,2},{3,19},{19,3},{4,20},{20... | collective-permute-start | bytes 16515080 | tf_op jit(solution)/shard_map/ppermute | solution.py:15
  162.0 19.5 %collective-permute-start.1 = (bf16[768,512]{1,0:T(8,128)(2,1)S(1)}, bf16[768,512]{1,0:T(8,128)(2,1)S(1)}, u32[]{:S(2)}, u32[]{:S(2)}) collective-permute-start(bf16[768,512]{1,0:T(8,128)(2,1)S(1)} %constant_dynamic-slice_fusion), channel_id=1, source_target_pairs={{0,16},{16,0},{1,17},{17,1},{2,18},{18,2},{3,19},{19,3},{4,20},{20... | collective-permute-start | bytes 2359304 | tf_op jit(solution)/shard_map/ppermute | solution.py:15
  181.4 20.0 %collective-permute-start.2 = (bf16[768,512]{1,0:T(8,128)(2,1)S(1)}, bf16[768,512]{1,0:T(8,128)(2,1)S(1)}, u32[]{:S(2)}, u32[]{:S(2)}) collective-permute-start(bf16[768,512]{1,0:T(8,128)(2,1)S(1)} %collective-permute-done.1), channel_id=1, source_target_pairs={{0,1},{1,2},{2,3},{3,0},{4,5},{5,6},{6,7},{7,4},{8,9},{9,10},{10,1... | collective-permute-start | bytes 2359304 | tf_op jit(solution)/shard_map/ppermute | solution.py:75
  182.0 35.0 %collective-permute-start.3 = (bf16[768,512]{1,0:T(8,128)(2,1)S(1)}, bf16[768,512]{1,0:T(8,128)(2,1)}, u32[]{:S(2)}, u32[]{:S(2)}) collective-permute-start(bf16[768,512]{1,0:T(8,128)(2,1)S(1)} %collective-permute-done.1), channel_id=1, source_target_pairs={{0,3},{1,0},{2,1},{3,2},{4,7},{5,4},{6,5},{7,6},{8,11},{9,8},{10,9... | collective-permute-start | bytes 2359304 | tf_op jit(solution)/shard_map/ppermute | solution.py:78
  201.4 32.7 %collective-permute-start.4 = (bf16[768,512]{1,0:T(8,128)(2,1)S(1)}, bf16[768,512]{1,0:T(8,128)(2,1)S(1)}, u32[]{:S(2)}, u32[]{:S(2)}) collective-permute-start(bf16[768,512]{1,0:T(8,128)(2,1)S(1)} %collective-permute-done.2), channel_id=1, source_target_pairs={{0,1},{1,2},{2,3},{3,0},{4,5},{5,6},{6,7},{7,4},{8,9},{9,10},{10,1... | collective-permute-start | bytes 2359304 | tf_op jit(solution)/shard_map/ppermute | solution.py:75
  234.3 18.4 %copy-start.2 = (bf16[768,2048]{1,0:T(8,128)(2,1)}, bf16[768,2048]{1,0:T(8,128)(2,1)S(1)}, u32[]{:S(2)}) copy-start(bf16[768,2048]{1,0:T(8,128)(2,1)S(1)} %constant_dynamic-update-slice_fusion) | copy-start | bytes 9437188
  234.3 20.1 %copy-start.4 = (bf16[256,2]{0,1:T(2,128)(2,1)S(1)}, bf16[256,2]{0,1:T(2,128)(2,1)}, u32[]{:S(2)}) copy-start(bf16[256,2]{0,1:T(2,128)(2,1)} %param.8) | copy-start | bytes 3076
  252.7 289.6 %collective-permute-start.5 = (f32[768,3584]{1,0:T(8,128)}, f32[768,3584]{1,0:T(8,128)}, u32[]{:S(2)}, u32[]{:S(2)}) collective-permute-start(f32[768,3584]{1,0:T(8,128)} %fusion.1), channel_id=1, source_target_pairs={{0,16},{16,0},{1,17},{17,1},{2,18},{18,2},{3,19},{19,3},{4,20},{20... | collective-permute-start | bytes 33030152 | tf_op jit(solution)/shard_map/ppermute | solution.py:15
  263.4 225.3 %collective-permute-start.6 = (bf16[768]{0:T(1024)(128)(2,1)S(1)}, bf16[768]{0:T(1024)(128)(2,1)S(1)}, u32[]{:S(2)}, u32[]{:S(2)}) collective-permute-start(bf16[768]{0:T(1024)(128)(2,1)S(1)} %reshape.71), channel_id=1, source_target_pairs={{0,16},{16,0},{1,17},{17,1},{2,18},{18,2},{3,19},{19,3},{4,20},{20... | collective-permute-start | bytes 4616 | tf_op jit(solution)/shard_map/ppermute | solution.py:15
  488.7 53.6 %slice-start = ((s8[5505024]{0:T(1024)(128)(4,1)}), s8[4194304]{0:T(1024)(128)(4,1)S(1)}, s32[]{:S(2)}) async-start(s8[5505024]{0:T(1024)(128)(4,1)} %bitcast.58), calls=%async_computation.4 | async-start | bytes 8388608
  507.0 18.4 %copy-start.3 = (bf16[768,2048]{1,0:T(8,128)(2,1)S(1)}, bf16[768,2048]{1,0:T(8,128)(2,1)}, u32[]{:S(2)}) copy-start(bf16[768,2048]{1,0:T(8,128)(2,1)} %copy-done.2) | copy-start | bytes 9437188
  507.0 35.3 %slice-start.1 = ((s8[5505024]{0:T(1024)(128)(4,1)}), s8[1310720]{0:T(1024)(128)(4,1)S(1)}, s32[]{:S(2)}) async-start(s8[5505024]{0:T(1024)(128)(4,1)} %bitcast.58), calls=%async_computation.5 | async-start | bytes 2621440
  567.4 27.1 %all-to-all-start.2 = ((f32[4,1,192]{2,1,0:T(1,128)}), f32[4,1,192]{2,1,0:T(1,128)S(1)}, u32[]{:S(2)}, u32[]{:S(2)}) async-start(f32[4,1,192]{2,1,0:T(1,128)} %psum.7), calls=%async_computation.2 | async-start | bytes 8192 | tf_op jit(solution)/shard_map/all_to_all | solution.py:117
  575.9 19.7 %copy-start.1 = (bf16[256,1024]{1,0:T(8,128)(2,1)S(1)}, bf16[256,1024]{1,0:T(8,128)(2,1)}, u32[]{:S(2)}) copy-start(bf16[256,1024]{1,0:T(8,128)(2,1)} %param.6) | copy-start | bytes 1572868
Sparse Core Ops, SparseCore 0:
  44.1 116.7 all-gather.1
